TPU v7x, 512 devices: a whole 4x8x8 slice. The times are simulated.
512 devices in a mesh: dp: 8 (over z_hi, core), seq: 64 (over x, z_lo, y).
Axes of the slice: x: 4, y: 8, z: 8 (z_hi: 4, z_lo: 2; z = z_hi * 2 + z_lo), core: 2. Of those that a mesh axis runs over, the one named last changes fastest.
Arguments:
- y_first: bfloat16 [8, 128, 64, 1152], P('dp', 'seq'), may hold values from -10 to 10
- y_second: bfloat16 [8, 128, 64, 1152], P('dp', 'seq'), may hold values from -10 to 10
- grad_first: bfloat16 [8, 128, 64, 1152], P('dp', 'seq'), may hold values from -6 to 6
- grad_second: bfloat16 [8, 128, 64, 1152], P('dp', 'seq'), may hold values from -6 to 6
- w_qkv_space: bfloat16 [1152, 1728], P('seq', 'dp'), may hold values from -1 to 1
- w_out_space: bfloat16 [576, 1152], P('seq', 'dp'), may hold values from -0.25 to 0.25
- w_qkv_time: bfloat16 [1152, 1728], P('seq', 'dp'), may hold values from -1 to 1
- w_out_time: bfloat16 [576, 1152], P('seq', 'dp'), may hold values from -0.25 to 0.25
Outputs:
- x_first: bfloat16 [8, 128, 64, 1152], P('dp', 'seq')
- x_second: bfloat16 [8, 128, 64, 1152], P('dp', 'seq')
- d_first: bfloat16 [8, 128, 64, 1152], P('dp', 'seq')
- d_second: bfloat16 [8, 128, 64, 1152], P('dp', 'seq')
- grad_w_out_time: float32 [576, 1152], P('seq', 'dp')
All inputs are finite; a program needn't handle non-finite values.
Results may differ from a plain program's by a relative error of at most 0.025.
Values may be sent and summed in bfloat16 or wider, within the bound.
No kernel may reach another device: no remote copies, remote signals or barrier semaphores. Data moves between devices by JAX's collectives and lax.ppermute only.
A program may use at most 64 MiB of HBM per device.

v0:
```python
import math
import jax
import jax.numpy as jnp
from jax import lax
from jax.sharding import PartitionSpec as P

HEADS = 8
HD = 72


def for_sending(shard):

    def short(part):
        return part.astype(jnp.bfloat16) if part.dtype == jnp.float32 else part

    return jax.tree.map(short, shard)


def normalize(values):
    wide = values.astype(jnp.float32)
    scale = lax.rsqrt(jnp.mean(wide * wide, axis=-1, keepdims=True) + 1e-06)
    return (wide * scale).astype(jnp.bfloat16)


def attend(inputs, w_qkv, w_out):
    outer, rows, inner, width = inputs.shape
    normed = normalize(inputs).reshape(-1, width)
    packed = jnp.dot(normed, w_qkv, preferred_element_type=jnp.float32).astype(jnp.bfloat16)
    packed = packed.reshape(outer, rows, inner, 3, HEADS, HD)
    query = packed[:, :, :, 0]
    keys = packed[:, :, :, 1]
    values = packed[:, :, :, 2]
    scores = jnp.einsum(
        "arbhk,asbhk->abhrs", query, keys, preferred_element_type=jnp.float32
    ) / math.sqrt(HD)
    peak = jnp.max(scores, axis=-1, keepdims=True)
    expo = jnp.exp(scores - peak)
    probs = (expo / jnp.sum(expo, axis=-1, keepdims=True)).astype(jnp.bfloat16)
    mixed = jnp.einsum(
        "abhrs,asbhk->arbhk", probs, values, preferred_element_type=jnp.float32
    ).astype(jnp.bfloat16)
    mixed = mixed.reshape(outer, rows, inner, HEADS * HD)
    result = jnp.dot(
        mixed.reshape(-1, HEADS * HD), w_out, preferred_element_type=jnp.float32
    ).astype(jnp.bfloat16)
    return (result.reshape(inputs.shape), mixed)


def body(
    y_first, y_second, grad_first, grad_second, w_qkv_space, w_out_space, w_qkv_time, w_out_time
):
    part_a, part_b, part_c, part_d = (
        lax.all_gather(w_qkv_space, "seq", axis=0, tiled=True),
        lax.all_gather(w_out_space, "seq", axis=0, tiled=True),
        lax.all_gather(w_qkv_time, "seq", axis=0, tiled=True),
        lax.all_gather(w_out_time, "seq", axis=0, tiled=True),
    )
    space_qkv, space_proj, time_qkv, time_proj = (
        lax.all_gather(part_a, "dp", axis=1, tiled=True),
        lax.all_gather(part_b, "dp", axis=1, tiled=True),
        lax.all_gather(part_c, "dp", axis=1, tiled=True),
        lax.all_gather(part_d, "dp", axis=1, tiled=True),
    )
    frame_count = y_first.shape[1]
    tokens = y_first.shape[2]
    width = y_first.shape[3]

    def time_fn(inputs):
        return attend(inputs, time_qkv, time_proj)

    def space_fn(inputs):
        return attend(inputs, space_qkv, space_proj)[0]

    first_patch = lax.all_to_all(y_first, "seq", split_axis=2, concat_axis=1, tiled=True)
    time_out, time_vjp, time_mixed = jax.vjp(time_fn, first_patch, has_aux=True)
    time_frames = jax.tree.map(
        lambda part, own: part.astype(own.dtype),
        lax.all_to_all(for_sending(time_out), "seq", split_axis=1, concat_axis=2, tiled=True),
        time_out,
    )
    second_in = (y_second.astype(jnp.float32) - time_frames.astype(jnp.float32)).astype(
        jnp.bfloat16
    )
    space_out, space_vjp = jax.vjp(space_fn, second_in.reshape(frame_count, tokens, 1, width))
    first_in = (
        y_first.astype(jnp.float32) - space_out.reshape(y_first.shape).astype(jnp.float32)
    ).astype(jnp.bfloat16)
    cot_patch = lax.all_to_all(grad_second, "seq", split_axis=2, concat_axis=1, tiled=True)
    back_patch = time_vjp(cot_patch)[0]
    back_frames = jax.tree.map(
        lambda part, own: part.astype(own.dtype),
        lax.all_to_all(for_sending(back_patch), "seq", split_axis=1, concat_axis=2, tiled=True),
        back_patch,
    )
    first_grad = (grad_first.astype(jnp.float32) + back_frames.astype(jnp.float32)).astype(
        jnp.bfloat16
    )
    back_space = space_vjp(first_grad.reshape(frame_count, tokens, 1, width))[0]
    second_grad = (
        grad_second.astype(jnp.float32) + back_space.reshape(y_first.shape).astype(jnp.float32)
    ).astype(jnp.bfloat16)
    partial_grad = lax.dot_general(
        time_mixed.reshape(-1, time_mixed.shape[3]),
        cot_patch.reshape(-1, width),
        (((0,), (0,)), ((), ())),
        preferred_element_type=jnp.float32,
    )
    row_share = lax.psum_scatter(partial_grad, "seq", scatter_dimension=0, tiled=True)
    grad_share = lax.psum_scatter(
        row_share.astype(jnp.bfloat16), "dp", scatter_dimension=1, tiled=True
    ).astype(jnp.float32)
    return (first_in, second_in, first_grad, second_grad, grad_share)


def solution(mesh):
    placed = (
        P("dp", "seq", None, None),
        P("dp", "seq", None, None),
        P("dp", "seq", None, None),
        P("dp", "seq", None, None),
        P("seq", "dp"),
        P("seq", "dp"),
        P("seq", "dp"),
        P("seq", "dp"),
    )
    return jax.shard_map(
        body,
        mesh=mesh,
        in_specs=placed,
        out_specs=(
            P("dp", "seq", None, None),
            P("dp", "seq", None, None),
            P("dp", "seq", None, None),
            P("dp", "seq", None, None),
            P("seq", "dp"),
        ),
        check_vma=False,
    )
```

profile of v0, /device:TPU:1, one launch (start us, length us, event | category | flops | bytes accessed | tf_op | source)
XLA Modules:
  0.0 1113.6 jit_solution(6876074772628245804)
XLA Ops:
  7.2 133.8 %all-gather.1 = bf16[64,9,144]{2,1,0:T(8,128)(2,1)S(1)} all-gather(bf16[1,9,144]{2,1,0:T(8,128)(2,1)} %bitcast.214), channel_id=1, replica_groups=mesh['dp'=8,'seq'=64] {'seq'}, dimensions={0}, use_global_device_ids=true | all-gather | bytes 168480 | tf_op jit(solution)/shard_map/all_gather | solution.py:56
  141.2 0.8 copy.137
  142.1 127.3 %all-gather = bf16[64,18,216]{2,1,0:T(8,128)(2,1)S(1)} all-gather(bf16[1,18,216]{2,1,0:T(8,128)(2,1)} %bitcast.212), channel_id=1, replica_groups=mesh['dp'=8,'seq'=64] {'seq'}, dimensions={0}, use_global_device_ids=true | all-gather | bytes 505440 | tf_op jit(solution)/shard_map/all_gather | solution.py:55
  269.4 0.3 reshape.509
  269.7 1.0 copy.135
  270.8 1.0 copy.132
  271.8 4.6 all-to-all-start
  276.4 1.0 copy.148
  277.4 1.3 dynamic-slice
  279.4 8.3 all-to-all-done
  287.7 4.6 all-to-all-start.2
  292.6 0.4 reshape.497
  293.0 0.4 fusion.12
  293.8 9.9 all-to-all-done.2
  303.8 2.0 convolution_convert_fusion.17
  305.8 75.2 %all-gather.9.cloned.1.call-done = bf16[1152,1728]{0,1:T(8,128)(2,1)} async-done(((bf16[1152,216]{0,1:T(8,128)(2,1)}), bf16[1152,1728]{0,1:T(8,128)(2,1)}) %all-gather.9.cloned.1.call-update) | async-done | bytes 3981328 | tf_op jit(solution)/shard_map/all_gather | solution.py:61
  381.0 3.4 convolution_convert_fusion.3
  384.4 0.3 fusion.58
  384.8 1.6 convert_reduce_fusion.1
  386.5 1.0 fusion.55
  387.7 0.5 copy-done.6
  388.1 0.7 copy-done.8
  388.8 0.5 fusion.60
  389.3 287.2 %all-reduce.8 = bf16[576,1152]{1,0:T(8,128)(2,1)} all-reduce(f32[576,1152]{1,0:T(8,128)S(1)} %fusion.60), channel_id=2, replica_groups=mesh['dp'=8,'seq'=64] {'seq'}, use_global_device_ids=true, to_apply=%region_14.0.clone | all-reduce | flops 663552 | bytes 3981312
  676.5 0.8 dynamic-slice_convert_fusion
  677.3 0.9 copy.165
  678.3 125.7 %all-gather.3 = bf16[64,9,144]{2,1,0:T(8,128)(2,1)S(1)} all-gather(bf16[1,9,144]{2,1,0:T(8,128)(2,1)} %bitcast.215), channel_id=1, replica_groups=mesh['dp'=8,'seq'=64] {'seq'}, dimensions={0}, use_global_device_ids=true | all-gather | bytes 168480 | tf_op jit(solution)/shard_map/all_gather | solution.py:54
  804.2 0.8 copy.147
  805.1 129.5 %all-gather.2 = bf16[64,18,216]{2,1,0:T(8,128)(2,1)S(1)} all-gather(bf16[1,18,216]{2,1,0:T(8,128)(2,1)S(1)} %bitcast.213), channel_id=1, replica_groups=mesh['dp'=8,'seq'=64] {'seq'}, dimensions={0}, use_global_device_ids=true | all-gather | bytes 505440 | tf_op jit(solution)/shard_map/all_gather | solution.py:53
  934.7 0.3 reshape.513
  935.0 1.0 copy.140
  936.0 0.3 fusion.9
  936.7 0.3 fusion.10
  937.0 3.0 multiply_reduce_fusion
  940.3 0.5 copy.184
  940.8 0.5 broadcast.221
  941.3 2.4 reduce.29
  943.7 0.8 reshape.522
  944.5 4.6 all-to-all-start.3
  949.2 0.6 fusion.2
  949.8 0.5 copy.185
  950.2 2.4 reduce.28
  952.6 0.8 reshape.520
  953.5 0.8 copy.166
  954.3 0.6 convert_element_type.411
  954.9 5.3 all-to-all-done.3
  960.3 5.6 all-to-all-start.1
  966.1 0.6 convert.16
  966.9 2.2 convolution_convert_fusion.16
  969.5 7.3 all-to-all-done.1
  977.0 0.6 convert.14
  978.0 115.5 %all-gather.13.cloned.1.call-done = bf16[1152,1728]{0,1:T(8,128)(2,1)} async-done(((bf16[1152,216]{0,1:T(8,128)(2,1)}), bf16[1152,1728]{0,1:T(8,128)(2,1)}) %all-gather.13.cloned.1.call-update) | async-done | bytes 3981328 | tf_op jit(solution)/shard_map/all_gather | solution.py:59
  1093.5 3.3 convolution_convert_fusion.2
  1096.9 0.4 reshape.519
  1097.2 0.6 fusion.57
  1098.3 0.3 fusion.59
  1099.1 0.3 convert_reduce_fusion
  1099.9 0.3 fusion.8
  1100.2 0.3 fusion.5
  1100.7 0.5 copy.158
  1101.2 0.5 reshape.496
  1101.8 3.0 fusion
  1105.4 0.6 convolution_convert_fusion.4
  1106.0 1.1 fusion.16
  (105 shorter events, 5.8 us)
Async XLA Ops:
  7.2 296.6 %all-gather.11.cloned.1.call-start = ((), (), s32[]{:S(2)}) async-start(), calls=%async_computation.6 | async-start | bytes 1658880 | tf_op jit(solution)/shard_map/all_gather | solution.py:62
  141.0 129.8 %copy-start.10 = (bf16[1,2,64,1152]{3,2,1,0:T(8,128)(2,1)S(1)}, bf16[1,2,64,1152]{3,2,1,0:T(8,128)(2,1)}, u32[]{:S(2)}) copy-start(bf16[1,2,64,1152]{3,2,1,0:T(8,128)(2,1)} %param.8) | copy-start | bytes 884740
  142.0 134.4 %copy-start.12 = (bf16[1,2,64,1152]{3,2,1,0:T(8,128)(2,1)S(1)}, bf16[1,2,64,1152]{3,2,1,0:T(8,128)(2,1)}, u32[]{:S(2)}) copy-start(bf16[1,2,64,1152]{3,2,1,0:T(8,128)(2,1)} %param.11) | copy-start | bytes 884740
  142.0 239.0 %all-gather.9.cloned.1.call-start = ((), (), s32[]{:S(2)}) async-start(), calls=%async_computation.5 | async-start | bytes 4478976 | tf_op jit(solution)/shard_map/all_gather | solution.py:61
  271.8 15.9 %all-to-all-start = ((bf16[1,2,64,1152]{3,1,0,2:T(2,128)(2,1)}), bf16[1,2,64,1152]{3,1,0,2:T(2,128)(2,1)S(1)}, u32[]{:S(2)}, u32[]{:S(2)}) async-start(bf16[1,2,64,1152]{3,1,0,2:T(2,128)(2,1)} %copy.132), calls=%async_computation | async-start | bytes 589824 | tf_op jit(solution)/shard_map/all_to_all | solution.py:74
  287.7 15.9 %all-to-all-start.2 = ((bf16[1,2,64,1152]{3,1,0,2:T(2,128)(2,1)}), bf16[1,2,64,1152]{3,1,0,2:T(2,128)(2,1)S(1)}, u32[]{:S(2)}, u32[]{:S(2)}) async-start(bf16[1,2,64,1152]{3,1,0,2:T(2,128)(2,1)} %copy.148), calls=%async_computation.2 | async-start | bytes 589824 | tf_op jit(solution)/shard_map/all_to_all | solution.py:88
  292.3 661.1 %reduce-scatter.4.cloned.1.call-start = ((), (), s32[]{:S(2)}) async-start(), calls=%async_computation.9 | async-start | bytes 331776
  293.7 9.9 copy-start.24
  293.7 90.7 %copy-start.22 = (f32[128]{0:T(128)}, f32[128]{0:T(128)S(1)}, u32[]{:S(2)}) copy-start(f32[128]{0:T(128)S(1)} %rsqrt.26) | copy-start | bytes 1540
  305.8 79.0 %copy-start.15 = (bf16[128,576]{0,1:T(8,128)(2,1)}, bf16[128,576]{0,1:T(8,128)(2,1)S(1)}, u32[]{:S(2)}) copy-start(bf16[128,576]{0,1:T(8,128)(2,1)S(1)} %convolution_convert_fusion.17) | copy-start | bytes 442372
  384.4 3.3 copy-start.4
  387.4 0.7 copy-start.6
  388.1 0.7 copy-start.8
  389.3 415.9 %copy-start.20 = (bf16[18,216]{1,0:T(8,128)(2,1)S(1)}, bf16[18,216]{1,0:T(8,128)(2,1)}, u32[]{:S(2)}) copy-start(bf16[18,216]{1,0:T(8,128)(2,1)} %param.12) | copy-start | bytes 23332
  678.2 288.6 %all-gather.15.cloned.1.call-start = ((), (), s32[]{:S(2)}) async-start(), calls=%async_computation.8 | async-start | bytes 1658880 | tf_op jit(solution)/shard_map/all_gather | solution.py:60
  804.0 132.1 %copy-start.7 = (bf16[8,128,128]{1,2,0:T(8,128)(2,1)S(1)}, bf16[8,128,128]{1,2,0:T(8,128)(2,1)}, u32[]{:S(2)}) copy-start(bf16[8,128,128]{1,2,0:T(8,128)(2,1)} %copy-done.6) | copy-start | bytes 786436
  804.0 132.1 %copy-start.16 = (bf16[128,576]{0,1:T(8,128)(2,1)S(1)}, bf16[128,576]{0,1:T(8,128)(2,1)}, u32[]{:S(2)}) copy-start(bf16[128,576]{0,1:T(8,128)(2,1)} %copy-done.15) | copy-start | bytes 442372
  804.2 132.1 %copy-start.21 = (f32[8,128]{1,0:T(8,128)S(1)}, f32[8,128]{1,0:T(8,128)}, u32[]{:S(2)}) copy-start(f32[8,128]{1,0:T(8,128)} %get-tuple-element.11) | copy-start | bytes 12292
  804.2 132.2 %copy-start.2 = (f32[8,128,128]{1,2,0:T(8,128)S(1)}, f32[8,128,128]{1,2,0:T(8,128)}, u32[]{:S(2)}) copy-start(f32[8,128,128]{1,2,0:T(8,128)} %get-tuple-element.10) | copy-start | bytes 1572868
  804.2 132.2 %copy-start.5 = (bf16[128,1728]{0,1:T(8,128)(2,1)S(1)}, bf16[128,1728]{0,1:T(8,128)(2,1)}, u32[]{:S(2)}) copy-start(bf16[128,1728]{0,1:T(8,128)(2,1)} %copy-done.4) | copy-start | bytes 1327108
  804.2 132.2 %copy-start.17 = (pred[8,128,128]{1,2,0:T(32,128)(4,1)S(1)}, pred[8,128,128]{1,2,0:T(32,128)(4,1)}, u32[]{:S(2)}) copy-start(pred[8,128,128]{1,2,0:T(32,128)(4,1)} %get-tuple-element.12) | copy-start | bytes 393220
  805.1 288.4 %all-gather.13.cloned.1.call-start = ((), (), s32[]{:S(2)}) async-start(), calls=%async_computation.7 | async-start | bytes 4478976 | tf_op jit(solution)/shard_map/all_gather | solution.py:59
  937.0 3.1 copy-start.25
  937.0 3.1 copy-start.23
  940.1 9.1 copy-start.1
  940.1 9.1 copy-start.9
  944.5 15.8 %all-to-all-start.3 = ((bf16[64,2,1152]{2,1,0:T(2,128)(2,1)}), bf16[64,2,1152]{2,1,0:T(2,128)(2,1)S(1)}, u32[]{:S(2)}, u32[]{:S(2)}) async-start(bf16[64,2,1152]{2,1,0:T(2,128)(2,1)} %reshape.522), calls=%async_computation.3 | async-start | bytes 589824 | tf_op jit(solution)/shard_map/all_to_all | solution.py:92
  949.8 17.0 %copy-start.18 = (bf16[1,2,64,1152]{3,2,1,0:T(8,128)(2,1)S(1)}, bf16[1,2,64,1152]{3,2,1,0:T(8,128)(2,1)}, u32[]{:S(2)}) copy-start(bf16[1,2,64,1152]{3,2,1,0:T(8,128)(2,1)} %param.10) | copy-start | bytes 884740
  960.3 16.5 %all-to-all-start.1 = ((bf16[64,2,1152]{2,1,0:T(2,128)(2,1)}), bf16[64,2,1152]{2,1,0:T(2,128)(2,1)S(1)}, u32[]{:S(2)}, u32[]{:S(2)}) async-start(bf16[64,2,1152]{2,1,0:T(2,128)(2,1)} %reshape.520), calls=%async_computation.1 | async-start | bytes 589824 | tf_op jit(solution)/shard_map/all_to_all | solution.py:78
  966.8 11.0 copy-start.14
  966.8 10.8 copy-start.19
  977.8 128.1 %copy-start.3 = (bf16[1,2,64,1152]{3,2,1,0:T(8,128)(2,1)}, bf16[1,2,64,1152]{3,2,1,0:T(8,128)(2,1)S(1)}, u32[]{:S(2)}) copy-start(bf16[1,2,64,1152]{3,2,1,0:T(8,128)(2,1)S(1)} %get-tuple-element.14) | copy-start | bytes 884740
  1101.8 3.6 copy-start
  1104.8 1.1 copy-start.11
  1104.8 1.1 copy-start.13
Sparse Core Ops, SparseCore 0:
  142.2 59.9 all-gather.10
  270.9 110.1 all-gather.8
  678.4 83.5 reduce-scatter.3
  805.2 108.5 all-gather.14
  936.1 157.3 all-gather.12
where the time goes:
time: 1110 us
  blocking collectives  803 us (72%)
  waiting for transfers between devices  222 us (20%)
  matrix products  23.2 us (2%)
  local copies, waits for them, and re-layouts  19.8 us (2%)
  starting transfers between devices  19.7 us (2%)
  between operations  15.2 us (1%)
    unnamed x1, blocking collectives  287 us
    all_gather x1, blocking collectives, body(): lax.all_gather(w_out_time, 'seq', axis=0, tiled=True)  134 us
    all_gather x1, blocking collectives, body(): lax.all_gather(w_qkv_space, 'seq', axis=0, tiled=True)  130 us
    all_gather x1, blocking collectives, body(): lax.all_gather(w_qkv_time, 'seq', axis=0, tiled=True)  127 us
    all_gather x1, blocking collectives, body(): lax.all_gather(w_out_space, 'seq', axis=0, tiled=True)  126 us
    all_gather x1, waiting for transfers between devices, body(): lax.all_gather(part_a, 'dp', axis=1, tiled=True)  115 us
    all_gather x1, waiting for transfers between devices, body(): lax.all_gather(part_c, 'dp', axis=1, tiled=True)  75.2 us
  transfers between devices with their start and end apart: 9, of which 6 were waited for; matrix products, arithmetic and copies ran while one was open for 3% of the time, Pallas kernels for 0%

commit v1 on v0

--- a/solution.py
+++ b/solution.py
@@ -52,7 +52,9 @@
     part_a, part_b, part_c, part_d = (
         lax.all_gather(w_qkv_space, "seq", axis=0, tiled=True),
         lax.all_gather(w_out_space, "seq", axis=0, tiled=True),
-        lax.all_gather(w_qkv_time, "seq", axis=0, tiled=True),
+        jnp.concatenate(
+            lax.all_to_all(jnp.stack([w_qkv_time] * lax.axis_size("seq")), "seq", 0, 0), axis=0
+        ),
         lax.all_gather(w_out_time, "seq", axis=0, tiled=True),
     )
     space_qkv, space_proj, time_qkv, time_proj = (

time: 1110 us -> 998 us (0.90)
  blocking collectives: 803 us -> 692 us
    all_gather x1 -> x0, blocking collectives: 127 us -> none  [body(): lax.all_gather(w_qkv_time, 'seq', axis=0, tiled=True)]
    all_gather x1, waiting for transfers between devices: 75.2 us -> 55.6 us  [body(): lax.all_gather(part_c, 'dp', axis=1, tiled=True)]
    all_to_all x0 -> x1, blocking collectives: none -> 19.4 us  [body(): lax.all_to_all(jnp.stack([w_qkv_time] * lax.axis_size('seq')), 'seq', 0, 0)]
  transfers between devices with their start and end apart: 9 -> 9, of which waited for: 6 -> 7; matrix products, arithmetic and copies ran while one was open for 3% -> 3% of each run, Pallas kernels for 0% -> 0%
where the time goes in v1:
time: 998 us; the launch traced here: 997 us
  blocking collectives  692 us (69%)
  waiting for transfers between devices  215 us (22%)
  matrix products  23.2 us (2%)
  starting transfers between devices  20.6 us (2%)
  local copies, waits for them, and re-layouts  20.6 us (2%)
  between operations  15.2 us (2%)
  other arithmetic  10.6 us (1%)
    unnamed x1, blocking collectives  284 us
    all_gather x1, blocking collectives, body(): lax.all_gather(w_out_time, 'seq', axis=0, tiled=True)  134 us
    all_gather x1, blocking collectives, body(): lax.all_gather(w_qkv_space, 'seq', axis=0, tiled=True)  129 us
    all_gather x1, blocking collectives, body(): lax.all_gather(w_out_space, 'seq', axis=0, tiled=True)  126 us
    all_gather x1, waiting for transfers between devices, body(): lax.all_gather(part_a, 'dp', axis=1, tiled=True)  119 us
    all_gather x1, waiting for transfers between devices, body(): lax.all_gather(part_c, 'dp', axis=1, tiled=True)  55.6 us
  transfers between devices with their start and end apart: 9, of which 7 were waited for; matrix products, arithmetic and copies ran while one was open for 3% of the time, Pallas kernels for 0%

profile of v1, /device:TPU:1, one launch (start us, length us, event | category | flops | bytes accessed | tf_op | source)
XLA Modules:
  0.0 996.9 jit_solution(8830713037729927957)
XLA Ops:
  7.2 133.8 %all-gather = bf16[64,9,144]{2,1,0:T(8,128)(2,1)S(1)} all-gather(bf16[1,9,144]{2,1,0:T(8,128)(2,1)} %bitcast.212), channel_id=1, replica_groups=mesh['dp'=8,'seq'=64] {'seq'}, dimensions={0}, use_global_device_ids=true | all-gather | bytes 168480 | tf_op jit(solution)/shard_map/all_gather | solution.py:58
  141.2 0.8 copy.137
  142.1 0.8 stack.2
  142.9 19.4 %all_to_all.47 = bf16[64,18,216]{2,1,0:T(8,128)(2,1)S(1)} all-to-all(bf16[64,18,216]{2,1,0:T(8,128)(2,1)S(1)} %stack.2), channel_id=1, replica_groups=mesh['dp'=8,'seq'=64] {'seq'}, dimensions={0} | all-to-all | bytes 995328 | tf_op jit(solution)/shard_map/all_to_all | solution.py:56
  162.3 0.3 reshape.484
  162.7 1.0 copy.135
  163.7 1.0 copy.132
  164.7 5.6 all-to-all-start
  170.4 1.0 copy.148
  171.4 1.3 dynamic-slice
  173.3 8.3 all-to-all-done
  181.6 4.6 all-to-all-start.3
  186.5 0.4 reshape.503
  186.9 0.4 fusion.12
  187.7 9.8 all-to-all-done.3
  197.6 9.0 all-gather.10.cloned.1.call-done
  206.6 2.0 convolution_convert_fusion.17
  208.7 55.6 %all-gather.8.cloned.1.call-done = bf16[1152,1728]{0,1:T(8,128)(2,1)} async-done(((bf16[1152,216]{0,1:T(8,128)(2,1)}), bf16[1152,1728]{0,1:T(8,128)(2,1)}) %all-gather.8.cloned.1.call-update) | async-done | bytes 3981328 | tf_op jit(solution)/shard_map/all_gather | solution.py:63
  264.3 3.4 convolution_convert_fusion.3
  267.7 0.3 fusion.58
  268.1 1.6 convert_reduce_fusion.1
  269.7 1.0 fusion.55
  271.0 0.5 copy-done.6
  271.4 0.7 copy-done.8
  272.1 0.5 fusion.60
  272.6 284.1 %all-reduce.8 = bf16[576,1152]{1,0:T(8,128)(2,1)} all-reduce(f32[576,1152]{1,0:T(8,128)S(1)} %fusion.60), channel_id=2, replica_groups=mesh['dp'=8,'seq'=64] {'seq'}, use_global_device_ids=true, to_apply=%region_14.0.clone | all-reduce | flops 663552 | bytes 3981312
  556.6 0.8 dynamic-slice_convert_fusion
  557.5 0.9 copy.165
  558.5 125.6 %all-gather.2 = bf16[64,9,144]{2,1,0:T(8,128)(2,1)S(1)} all-gather(bf16[1,9,144]{2,1,0:T(8,128)(2,1)} %bitcast.213), channel_id=1, replica_groups=mesh['dp'=8,'seq'=64] {'seq'}, dimensions={0}, use_global_device_ids=true | all-gather | bytes 168480 | tf_op jit(solution)/shard_map/all_gather | solution.py:54
  684.3 0.8 copy.147
  685.2 128.9 %all-gather.1 = bf16[64,18,216]{2,1,0:T(8,128)(2,1)S(1)} all-gather(bf16[1,18,216]{2,1,0:T(8,128)(2,1)S(1)} %bitcast.211), channel_id=1, replica_groups=mesh['dp'=8,'seq'=64] {'seq'}, dimensions={0}, use_global_device_ids=true | all-gather | bytes 505440 | tf_op jit(solution)/shard_map/all_gather | solution.py:53
  814.1 0.3 reshape.517
  814.4 1.0 copy.140
  815.5 0.3 fusion.9
  816.1 0.3 fusion.10
  816.5 3.0 multiply_reduce_fusion
  819.7 0.5 copy.184
  820.2 0.5 broadcast.223
  820.7 2.4 reduce.29
  823.1 0.8 reshape.526
  823.9 4.6 all-to-all-start.4
  828.6 0.6 fusion.2
  829.2 0.5 copy.185
  829.6 2.4 reduce.28
  832.0 0.8 reshape.524
  832.9 0.8 copy.166
  833.7 0.6 convert_element_type.411
  834.3 5.4 all-to-all-done.4
  839.8 5.5 all-to-all-start.2
  845.5 0.6 convert.16
  846.3 2.2 convolution_convert_fusion.16
  848.9 7.5 all-to-all-done.2
  856.7 0.6 convert.14
  857.7 119.2 %all-gather.12.cloned.1.call-done = bf16[1152,1728]{0,1:T(8,128)(2,1)} async-done(((bf16[1152,216]{0,1:T(8,128)(2,1)}), bf16[1152,1728]{0,1:T(8,128)(2,1)}) %all-gather.12.cloned.1.call-update) | async-done | bytes 3981328 | tf_op jit(solution)/shard_map/all_gather | solution.py:61
  976.9 3.3 convolution_convert_fusion.2
  980.2 0.4 reshape.523
  980.6 0.6 fusion.57
  982.4 0.3 convert_reduce_fusion
  983.2 0.3 fusion.8
  984.0 0.5 copy.158
  984.6 0.5 reshape.502
  985.1 3.0 fusion
  988.7 0.6 convolution_convert_fusion.4
  989.3 1.1 fusion.16
  (106 shorter events, 6.4 us)
Async XLA Ops:
  7.2 199.4 %all-gather.10.cloned.1.call-start = ((), (), s32[]{:S(2)}) async-start(), calls=%async_computation.7 | async-start | bytes 1658880 | tf_op jit(solution)/shard_map/all_gather | solution.py:64
  142.0 21.7 %copy-start.10 = (bf16[1,2,64,1152]{3,2,1,0:T(8,128)(2,1)S(1)}, bf16[1,2,64,1152]{3,2,1,0:T(8,128)(2,1)}, u32[]{:S(2)}) copy-start(bf16[1,2,64,1152]{3,2,1,0:T(8,128)(2,1)} %param.8) | copy-start | bytes 884740
  142.1 122.2 %all-gather.8.cloned.1.call-start = ((), (), s32[]{:S(2)}) async-start(), calls=%async_computation.6 | async-start | bytes 4478976 | tf_op jit(solution)/shard_map/all_gather | solution.py:63
  142.9 27.5 %copy-start.12 = (bf16[1,2,64,1152]{3,2,1,0:T(8,128)(2,1)S(1)}, bf16[1,2,64,1152]{3,2,1,0:T(8,128)(2,1)}, u32[]{:S(2)}) copy-start(bf16[1,2,64,1152]{3,2,1,0:T(8,128)(2,1)} %param.11) | copy-start | bytes 884740
  164.7 16.9 %all-to-all-start = ((bf16[1,2,64,1152]{3,1,0,2:T(2,128)(2,1)}), bf16[1,2,64,1152]{3,1,0,2:T(2,128)(2,1)S(1)}, u32[]{:S(2)}, u32[]{:S(2)}) async-start(bf16[1,2,64,1152]{3,1,0,2:T(2,128)(2,1)} %copy.132), calls=%async_computation | async-start | bytes 589824 | tf_op jit(solution)/shard_map/all_to_all | solution.py:76
  181.6 15.9 %all-to-all-start.3 = ((bf16[1,2,64,1152]{3,1,0,2:T(2,128)(2,1)}), bf16[1,2,64,1152]{3,1,0,2:T(2,128)(2,1)S(1)}, u32[]{:S(2)}, u32[]{:S(2)}) async-start(bf16[1,2,64,1152]{3,1,0,2:T(2,128)(2,1)} %copy.148), calls=%async_computation.3 | async-start | bytes 589824 | tf_op jit(solution)/shard_map/all_to_all | solution.py:90
  186.2 646.6 %reduce-scatter.4.cloned.1.call-start = ((), (), s32[]{:S(2)}) async-start(), calls=%async_computation.10 | async-start | bytes 331776
  187.6 9.9 copy-start.24
  187.6 80.0 %copy-start.22 = (f32[128]{0:T(128)}, f32[128]{0:T(128)S(1)}, u32[]{:S(2)}) copy-start(f32[128]{0:T(128)S(1)} %rsqrt.26) | copy-start | bytes 1540
  208.7 59.5 %copy-start.15 = (bf16[128,576]{0,1:T(8,128)(2,1)}, bf16[128,576]{0,1:T(8,128)(2,1)S(1)}, u32[]{:S(2)}) copy-start(bf16[128,576]{0,1:T(8,128)(2,1)S(1)} %convolution_convert_fusion.17) | copy-start | bytes 442372
  267.7 3.3 copy-start.4
  270.7 0.7 copy-start.6
  271.4 0.7 copy-start.8
  272.6 412.7 %copy-start.20 = (bf16[18,216]{1,0:T(8,128)(2,1)S(1)}, bf16[18,216]{1,0:T(8,128)(2,1)}, u32[]{:S(2)}) copy-start(bf16[18,216]{1,0:T(8,128)(2,1)} %param.12) | copy-start | bytes 23332
  558.4 287.9 %all-gather.14.cloned.1.call-start = ((), (), s32[]{:S(2)}) async-start(), calls=%async_computation.9 | async-start | bytes 1658880 | tf_op jit(solution)/shard_map/all_gather | solution.py:62
  684.0 131.4 %copy-start.7 = (bf16[8,128,128]{1,2,0:T(8,128)(2,1)S(1)}, bf16[8,128,128]{1,2,0:T(8,128)(2,1)}, u32[]{:S(2)}) copy-start(bf16[8,128,128]{1,2,0:T(8,128)(2,1)} %copy-done.6) | copy-start | bytes 786436
  684.0 131.4 %copy-start.16 = (bf16[128,576]{0,1:T(8,128)(2,1)S(1)}, bf16[128,576]{0,1:T(8,128)(2,1)}, u32[]{:S(2)}) copy-start(bf16[128,576]{0,1:T(8,128)(2,1)} %copy-done.15) | copy-start | bytes 442372
  684.3 131.5 %copy-start.21 = (f32[8,128]{1,0:T(8,128)S(1)}, f32[8,128]{1,0:T(8,128)}, u32[]{:S(2)}) copy-start(f32[8,128]{1,0:T(8,128)} %get-tuple-element.11) | copy-start | bytes 12292
  684.3 131.5 %copy-start.2 = (f32[8,128,128]{1,2,0:T(8,128)S(1)}, f32[8,128,128]{1,2,0:T(8,128)}, u32[]{:S(2)}) copy-start(f32[8,128,128]{1,2,0:T(8,128)} %get-tuple-element.10) | copy-start | bytes 1572868
  684.3 131.5 %copy-start.5 = (bf16[128,1728]{0,1:T(8,128)(2,1)S(1)}, bf16[128,1728]{0,1:T(8,128)(2,1)}, u32[]{:S(2)}) copy-start(bf16[128,1728]{0,1:T(8,128)(2,1)} %copy-done.4) | copy-start | bytes 1327108
  684.3 131.5 %copy-start.17 = (pred[8,128,128]{1,2,0:T(32,128)(4,1)S(1)}, pred[8,128,128]{1,2,0:T(32,128)(4,1)}, u32[]{:S(2)}) copy-start(pred[8,128,128]{1,2,0:T(32,128)(4,1)} %get-tuple-element.12) | copy-start | bytes 393220
  685.2 291.7 %all-gather.12.cloned.1.call-start = ((), (), s32[]{:S(2)}) async-start(), calls=%async_computation.8 | async-start | bytes 4478976 | tf_op jit(solution)/shard_map/all_gather | solution.py:61
  816.4 3.1 copy-start.25
  816.4 3.1 copy-start.23
  819.5 9.1 copy-start.1
  819.5 9.1 copy-start.9
  823.9 15.9 %all-to-all-start.4 = ((bf16[64,2,1152]{2,1,0:T(2,128)(2,1)}), bf16[64,2,1152]{2,1,0:T(2,128)(2,1)S(1)}, u32[]{:S(2)}, u32[]{:S(2)}) async-start(bf16[64,2,1152]{2,1,0:T(2,128)(2,1)} %reshape.526), calls=%async_computation.4 | async-start | bytes 589824 | tf_op jit(solution)/shard_map/all_to_all | solution.py:94
  829.2 17.0 %copy-start.18 = (bf16[1,2,64,1152]{3,2,1,0:T(8,128)(2,1)S(1)}, bf16[1,2,64,1152]{3,2,1,0:T(8,128)(2,1)}, u32[]{:S(2)}) copy-start(bf16[1,2,64,1152]{3,2,1,0:T(8,128)(2,1)} %param.10) | copy-start | bytes 884740
  839.8 16.6 %all-to-all-start.2 = ((bf16[64,2,1152]{2,1,0:T(2,128)(2,1)}), bf16[64,2,1152]{2,1,0:T(2,128)(2,1)S(1)}, u32[]{:S(2)}, u32[]{:S(2)}) async-start(bf16[64,2,1152]{2,1,0:T(2,128)(2,1)} %reshape.524), calls=%async_computation.2 | async-start | bytes 589824 | tf_op jit(solution)/shard_map/all_to_all | solution.py:80
  846.2 11.2 %copy-start.14 = (bf16[1,2,64,1152]{3,2,1,0:T(8,128)(2,1)}, bf16[1,2,64,1152]{3,2,1,0:T(8,128)(2,1)S(1)}, u32[]{:S(2)}) copy-start(bf16[1,2,64,1152]{3,2,1,0:T(8,128)(2,1)S(1)} %fusion.15) | copy-start | bytes 884740
  846.2 11.0 %copy-start.19 = (bf16[1,2,64,1152]{3,2,1,0:T(8,128)(2,1)S(1)}, bf16[1,2,64,1152]{3,2,1,0:T(8,128)(2,1)}, u32[]{:S(2)}) copy-start(bf16[1,2,64,1152]{3,2,1,0:T(8,128)(2,1)} %param.9) | copy-start | bytes 884740
  857.5 131.8 %copy-start.3 = (bf16[1,2,64,1152]{3,2,1,0:T(8,128)(2,1)}, bf16[1,2,64,1152]{3,2,1,0:T(8,128)(2,1)S(1)}, u32[]{:S(2)}) copy-start(bf16[1,2,64,1152]{3,2,1,0:T(8,128)(2,1)S(1)} %get-tuple-element.14) | copy-start | bytes 884740
  985.1 3.6 copy-start
  988.1 1.1 copy-start.11
  988.1 1.1 copy-start.13
Sparse Core Ops, SparseCore 0:
  142.2 64.4 all-gather.9
  208.8 55.4 all-gather.7
  558.5 86.4 reduce-scatter.3
  685.3 111.4 all-gather.13
  815.6 161.2 all-gather.11
